TPU v7x, 32 devices: a whole 2x2x4 slice. The times are simulated.
32 devices in a mesh: gx: 4 (over y, x), gy: 8 (over z, core).
Axes of the slice: x: 2, y: 2, z: 4, core: 2. Of those that a mesh axis runs over, the one named last changes fastest.
Arguments:
- start_field: float32 [64, 64, 512], P('gx', 'gy'), may hold values from -6 to 6
- right_side: float32 [64, 64, 512], P('gx', 'gy'), may hold values from -12 to 12
- accumulation: float32 [64, 64, 512], P('gx', 'gy'), may hold values from 0.05 to 1
- trans_x: float32 [64, 64, 512], P('gx', 'gy'), may hold values from 0.1 to 10
- trans_y: float32 [64, 64, 512], P('gx', 'gy'), may hold values from 0.1 to 10
- trans_z: float32 [64, 64, 512], P('gx', 'gy'), may hold values from 0.1 to 10
Outputs:
- ortho_basis: float32 [5, 64, 64, 512], P(None, 'gx', 'gy')
- upper_factor: float32 [5, 5], replicated
- residual_scale: float32 [], replicated
All inputs are finite; a program needn't handle non-finite values.
Results may differ from a plain program's by a relative error of at most 0.0003.
Values sent between devices are 32-bit elements; how exact they have to be, the bound alone decides.
No kernel may reach another device: no remote copies, remote signals or barrier semaphores. Data moves between devices by JAX's collectives and lax.ppermute only.
A program may use at most 64 MiB of HBM per device.

v0:
```python
import jax
import jax.numpy as jnp
from jax import lax
from jax.sharding import PartitionSpec as P

STEPS = 4
EPS = 1e-06


def padded(block, sides, width):
    for axis, dim in sides:
        count = lax.axis_size(axis)
        forward = [(i, i + 1) for i in range(count - 1)]
        backward = [(target, source) for source, target in forward]
        low = lax.ppermute(
            lax.slice_in_dim(block, block.shape[dim] - width, None, axis=dim), axis, forward
        )
        high = lax.ppermute(lax.slice_in_dim(block, 0, width, axis=dim), axis, backward)
        block = jnp.concatenate([low, block, high], axis=dim)
    return block


def from_behind(value, axis, by):
    peers = lax.axis_size(axis)
    pairs = [(i, i + by) for i in range(peers) if 0 <= i + by < peers]
    return lax.ppermute(value, axis, pairs)


def neighbours(field, coef):
    acc_c, t_x, t_y, t_z = coef
    lx = field.shape[0] - 2
    ly = field.shape[1] - 2
    ox = (t_x.shape[0] - lx) // 2
    oy = (t_x.shape[1] - ly) // 2

    def piece(a, dx, dy):
        return a[ox + dx : ox + dx + lx, oy + dy : oy + dy + ly]

    centre = field[1:-1, 1:-1]
    zero_plane = jnp.zeros_like(centre[..., :1])
    tz_low = piece(t_z, 0, 0)
    tz_high = jnp.concatenate([tz_low[..., 1:], zero_plane], axis=-1)
    z_low = jnp.concatenate([zero_plane, centre[..., :-1]], axis=-1)
    z_high = jnp.concatenate([centre[..., 1:], zero_plane], axis=-1)
    tx_low = piece(t_x, 0, 0)
    tx_high = piece(t_x, 1, 0)
    ty_low = piece(t_y, 0, 0)
    ty_high = piece(t_y, 0, 1)
    total = tx_low * field[:-2, 1:-1] + tx_high * field[2:, 1:-1]
    total = total + ty_low * field[1:-1, :-2] + ty_high * field[1:-1, 2:]
    total = total + tz_low * z_low + tz_high * z_high
    diagonal = piece(acc_c, 0, 0) + tx_low + tx_high + ty_low + ty_high + tz_low + tz_high
    return (total, diagonal)


def upper_inverse(upper):
    size = upper.shape[0]
    columns = []
    for col in range(size):
        values = [None] * size
        for row in reversed(range(size)):
            value = jnp.float32(1.0 if row == col else 0.0)
            for inner in range(row + 1, size):
                value = value - upper[row, inner] * values[inner]
            values[row] = value / upper[row, row]
        columns.append(jnp.stack(values))
    return jnp.stack(columns, axis=1)


def pad_plain(a):
    return jnp.pad(a, ((1, 1), (1, 1), (0, 0)))


def field_widen(field):
    return padded(field, (("gx", 0), ("gy", 1)), 1)


def local(start_field, right_side, accumulation, trans_x, trans_y, trans_z):
    size_x, size_y, size_z = start_field.shape
    cells = size_x * size_y * size_z * lax.axis_size("gx") * lax.axis_size("gy")
    plane_x = from_behind(trans_x[:1], "gx", -1)
    plane_y = from_behind(trans_y[:, :1], "gy", -1)
    rim_x = jnp.pad(jnp.concatenate([trans_x, plane_x], axis=0), ((1, 0), (1, 1), (0, 0)))
    rim_y = jnp.pad(jnp.concatenate([trans_y, plane_y], axis=1), ((1, 1), (1, 0), (0, 0)))
    coef = (pad_plain(accumulation), rim_x, rim_y, pad_plain(trans_z))
    total, diagonal = neighbours(field_widen(start_field), coef)
    residual0 = right_side - (diagonal * start_field - total)
    squares = lax.psum(jnp.sum(residual0 * residual0), ("gx", "gy"))
    scale = jnp.sqrt(squares / cells + EPS)
    vector = residual0 / scale
    basis = [residual0 / scale]
    for step in range(STEPS):
        total, diagonal = neighbours(field_widen(vector), coef)
        vector = 2.0 * total / diagonal
        basis.append(vector)
    block = jnp.stack(basis)
    local_gram = jnp.einsum("axyz,bxyz->ab", block, block, precision=lax.Precision.HIGHEST)
    gram = lax.psum(local_gram, ("gx", "gy")) / cells
    upper = jnp.linalg.cholesky(gram).T
    inverse = upper_inverse(upper)
    ortho = jnp.einsum("jk,jxyz->kxyz", inverse, block, precision=lax.Precision.HIGHEST)
    return (ortho, upper, scale)


def solution(mesh):
    in_specs = (
        P("gx", "gy", None),
        P("gx", "gy", None),
        P("gx", "gy", None),
        P("gx", "gy", None),
        P("gx", "gy", None),
        P("gx", "gy", None),
    )
    out_specs = (P(None, "gx", "gy", None), P(), P())
    return jax.shard_map(local, mesh=mesh, in_specs=in_specs, out_specs=out_specs, check_vma=False)
```

profile of v0, /device:TPU:0, one launch (start us, length us, event | category | flops | bytes accessed | tf_op | source)
XLA Modules:
  0.0 220.1 jit_solution(5682292001169341076)
XLA Ops:
  0.7 0.8 fusion.73
  1.5 4.8 %collective-permute-start.2 = (f32[1,8,512]{2,1,0:T(8,128)S(1)}, f32[1,8,512]{2,1,0:T(8,128)S(1)}, u32[]{:S(2)}, u32[]{:S(2)}) collective-permute-start(f32[1,8,512]{2,1,0:T(8,128)S(1)} %get-tuple-element.35), channel_id=1, source_target_pairs={{0,8},{8,16},{16,24},{1,9},{9,17},{17,25},{2,10},{10,18},{18,26},{... | collective-permute-start | bytes 49160 | tf_op jit(solution)/shard_map/ppermute | solution.py:15
  6.4 0.7 slice.332
  7.1 1.3 collective-permute-start
  8.4 1.3 collective-permute-start.3
  9.7 1.0 slice.334
  10.7 1.3 collective-permute-start.1
  12.0 1.0 constant_dynamic-update-slice_fusion.1
  13.0 1.7 collective-permute-done.3
  14.7 1.4 collective-permute-start.4
  16.1 1.3 collective-permute-start.5
  17.4 1.2 fusion.74
  18.7 2.2 %collective-permute-done.5 = f32[18,1,512]{2,1,0:T(1,128)S(1)} collective-permute-done((f32[18,1,512]{2,1,0:T(1,128)S(1)}, f32[18,1,512]{2,1,0:T(1,128)S(1)}, u32[]{:S(2)}, u32[]{:S(2)}) %collective-permute-start.5) | collective-permute-done | bytes 36896 | tf_op jit(solution)/shard_map/ppermute | solution.py:18
  21.0 1.0 multiply_reduce_fusion
  21.9 44.0 %psum.14 = f32[]{:T(128)} all-reduce(f32[]{:T(128)} %get-tuple-element.6), channel_id=1, replica_groups=mesh['gx'=4,'gy'=8] {'gx','gy'}, use_global_device_ids=true, to_apply=%region_1.2 | all-reduce | flops 1 | bytes 8 | tf_op jit(solution)/shard_map/psum | solution.py:88
  66.7 4.2 %collective-permute-start.6 = (f32[1,8,512]{2,1,0:T(8,128)S(1)}, f32[1,8,512]{2,1,0:T(8,128)S(1)}, u32[]{:S(2)}, u32[]{:S(2)}) collective-permute-start(f32[1,8,512]{2,1,0:T(8,128)S(1)} %get-tuple-element.32), channel_id=1, source_target_pairs={{0,8},{8,16},{16,24},{1,9},{9,17},{17,25},{2,10},{10,18},{18,26},{... | collective-permute-start | bytes 49160 | tf_op jit(solution)/shard_map/ppermute | solution.py:15
  70.9 1.3 collective-permute-start.7
  72.3 4.2 %collective-permute-done.7 = f32[1,8,512]{2,1,0:T(8,128)S(1)} collective-permute-done((f32[1,8,512]{2,1,0:T(8,128)S(1)}, f32[1,8,512]{2,1,0:T(8,128)S(1)}, u32[]{:S(2)}, u32[]{:S(2)}) %collective-permute-start.7) | collective-permute-done | bytes 16416 | tf_op jit(solution)/shard_map/ppermute | solution.py:18
  76.6 1.3 collective-permute-start.8
  77.9 1.3 collective-permute-start.9
  79.3 3.2 %collective-permute-done.9 = f32[18,1,512]{2,1,0:T(1,128)S(1)} collective-permute-done((f32[18,1,512]{2,1,0:T(1,128)S(1)}, f32[18,1,512]{2,1,0:T(1,128)S(1)}, u32[]{:S(2)}, u32[]{:S(2)}) %collective-permute-start.9) | collective-permute-done | bytes 36896 | tf_op jit(solution)/shard_map/ppermute | solution.py:18
  82.9 4.5 %collective-permute-start.10 = (f32[1,8,512]{2,1,0:T(8,128)S(1)}, f32[1,8,512]{2,1,0:T(8,128)S(1)}, u32[]{:S(2)}, u32[]{:S(2)}) collective-permute-start(f32[1,8,512]{2,1,0:T(8,128)S(1)} %get-tuple-element.28), channel_id=1, source_target_pairs={{0,8},{8,16},{16,24},{1,9},{9,17},{17,25},{2,10},{10,18},{18,26},{... | collective-permute-start | bytes 49160 | tf_op jit(solution)/shard_map/ppermute | solution.py:15
  87.4 1.3 collective-permute-start.11
  88.8 4.2 %collective-permute-done.11 = f32[1,8,512]{2,1,0:T(8,128)S(1)} collective-permute-done((f32[1,8,512]{2,1,0:T(8,128)S(1)}, f32[1,8,512]{2,1,0:T(8,128)S(1)}, u32[]{:S(2)}, u32[]{:S(2)}) %collective-permute-start.11) | collective-permute-done | bytes 16416 | tf_op jit(solution)/shard_map/ppermute | solution.py:18
  93.1 3.1 %collective-permute-start.12 = (f32[18,1,512]{2,1,0:T(1,128)S(1)}, f32[18,1,512]{2,1,0:T(1,128)S(1)}, u32[]{:S(2)}, u32[]{:S(2)}) collective-permute-start(f32[18,1,512]{2,1,0:T(1,128)S(1)} %get-tuple-element.12), channel_id=1, source_target_pairs={{0,1},{1,2},{2,3},{3,4},{4,5},{5,6},{6,7},{8,9},{9,10},{10,11},{11... | collective-permute-start | bytes 110600 | tf_op jit(solution)/shard_map/ppermute | solution.py:15
  96.2 1.3 collective-permute-start.13
  97.7 2.6 %collective-permute-done.13 = f32[18,1,512]{2,1,0:T(1,128)S(1)} collective-permute-done((f32[18,1,512]{2,1,0:T(1,128)S(1)}, f32[18,1,512]{2,1,0:T(1,128)S(1)}, u32[]{:S(2)}, u32[]{:S(2)}) %collective-permute-start.13) | collective-permute-done | bytes 36896 | tf_op jit(solution)/shard_map/ppermute | solution.py:18
  100.6 2.8 %collective-permute-start.14 = (f32[1,8,512]{2,1,0:T(8,128)S(1)}, f32[1,8,512]{2,1,0:T(8,128)S(1)}, u32[]{:S(2)}, u32[]{:S(2)}) collective-permute-start(f32[1,8,512]{2,1,0:T(8,128)S(1)} %get-tuple-element.24), channel_id=1, source_target_pairs={{0,8},{8,16},{16,24},{1,9},{9,17},{17,25},{2,10},{10,18},{18,26},{... | collective-permute-start | bytes 49160 | tf_op jit(solution)/shard_map/ppermute | solution.py:15
  103.5 1.3 collective-permute-start.15
  104.9 4.2 %collective-permute-done.15 = f32[1,8,512]{2,1,0:T(8,128)S(1)} collective-permute-done((f32[1,8,512]{2,1,0:T(8,128)S(1)}, f32[1,8,512]{2,1,0:T(8,128)S(1)}, u32[]{:S(2)}, u32[]{:S(2)}) %collective-permute-start.15) | collective-permute-done | bytes 16416 | tf_op jit(solution)/shard_map/ppermute | solution.py:18
  109.1 3.1 %collective-permute-start.16 = (f32[18,1,512]{2,1,0:T(1,128)S(1)}, f32[18,1,512]{2,1,0:T(1,128)S(1)}, u32[]{:S(2)}, u32[]{:S(2)}) collective-permute-start(f32[18,1,512]{2,1,0:T(1,128)S(1)} %get-tuple-element.10), channel_id=1, source_target_pairs={{0,1},{1,2},{2,3},{3,4},{4,5},{5,6},{6,7},{8,9},{9,10},{10,11},{11... | collective-permute-start | bytes 110600 | tf_op jit(solution)/shard_map/ppermute | solution.py:15
  112.3 1.3 collective-permute-start.17
  113.7 2.6 %collective-permute-done.17 = f32[18,1,512]{2,1,0:T(1,128)S(1)} collective-permute-done((f32[18,1,512]{2,1,0:T(1,128)S(1)}, f32[18,1,512]{2,1,0:T(1,128)S(1)}, u32[]{:S(2)}, u32[]{:S(2)}) %collective-permute-start.17) | collective-permute-done | bytes 36896 | tf_op jit(solution)/shard_map/ppermute | solution.py:18
  116.7 2.8 %collective-permute-start.18 = (f32[1,8,512]{2,1,0:T(8,128)S(1)}, f32[1,8,512]{2,1,0:T(8,128)S(1)}, u32[]{:S(2)}, u32[]{:S(2)}) collective-permute-start(f32[1,8,512]{2,1,0:T(8,128)S(1)} %get-tuple-element.20), channel_id=1, source_target_pairs={{0,8},{8,16},{16,24},{1,9},{9,17},{17,25},{2,10},{10,18},{18,26},{... | collective-permute-start | bytes 49160 | tf_op jit(solution)/shard_map/ppermute | solution.py:15
  119.5 1.3 collective-permute-start.19
  121.7 3.5 %collective-permute-done.19 = f32[1,8,512]{2,1,0:T(8,128)S(1)} collective-permute-done((f32[1,8,512]{2,1,0:T(8,128)S(1)}, f32[1,8,512]{2,1,0:T(8,128)S(1)}, u32[]{:S(2)}, u32[]{:S(2)}) %collective-permute-start.19) | collective-permute-done | bytes 16416 | tf_op jit(solution)/shard_map/ppermute | solution.py:18
  125.2 3.1 %collective-permute-start.20 = (f32[18,1,512]{2,1,0:T(1,128)S(1)}, f32[18,1,512]{2,1,0:T(1,128)S(1)}, u32[]{:S(2)}, u32[]{:S(2)}) collective-permute-start(f32[18,1,512]{2,1,0:T(1,128)S(1)} %get-tuple-element.8), channel_id=1, source_target_pairs={{0,1},{1,2},{2,3},{3,4},{4,5},{5,6},{6,7},{8,9},{9,10},{10,11},{11... | collective-permute-start | bytes 110600 | tf_op jit(solution)/shard_map/ppermute | solution.py:15
  128.4 1.3 collective-permute-start.21
  130.1 2.3 %collective-permute-done.21 = f32[18,1,512]{2,1,0:T(1,128)S(1)} collective-permute-done((f32[18,1,512]{2,1,0:T(1,128)S(1)}, f32[18,1,512]{2,1,0:T(1,128)S(1)}, u32[]{:S(2)}, u32[]{:S(2)}) %collective-permute-start.21) | collective-permute-done | bytes 36896 | tf_op jit(solution)/shard_map/ppermute | solution.py:18
  132.9 2.1 stack.119
  135.0 4.6 %convolution_bitcast_fusion = f32[5,5]{0,1:T(8,128)S(1)} fusion(f32[5,16,8,512]{3,0,2,1:T(8,128)S(1)} %stack.119), kind=kOutput, calls=%fused_computation | convolution fusion | flops 19660800 | bytes 1310820 | tf_op jit(solution)/shard_map/axyz,bxyz->ab/dot_general | solution.py:97
  139.6 40.9 %psum.15 = f32[5,5]{0,1:T(8,128)S(1)} all-reduce(f32[5,5]{0,1:T(8,128)S(1)} %convolution_bitcast_fusion), channel_id=1, replica_groups=mesh['gx'=4,'gy'=8] {'gx','gy'}, use_global_device_ids=true, to_apply=%region_2.3 | all-reduce | flops 25 | bytes 200 | tf_op jit(solution)/shard_map/psum | solution.py:98
  181.0 0.6 compare_reduce_fusion
  181.7 0.6 select_bitcast_fusion
  182.4 0.7 copy.16
  183.0 0.7 fusion.75
  215.3 1.8 fusion.60
  217.1 1.8 copy.15
  (62 shorter events, 5.1 us)
Async XLA Ops:
  0.6 20.3 %copy-start.4 = (f32[16,8,512]{2,1,0:T(8,128)S(1)}, f32[16,8,512]{2,1,0:T(8,128)}, u32[]{:S(2)}) copy-start(f32[16,8,512]{2,1,0:T(8,128)} %param.6) | copy-start | bytes 786436
  0.6 20.3 %copy-start.2 = (f32[16,8,512]{2,1,0:T(8,128)S(1)}, f32[16,8,512]{2,1,0:T(8,128)}, u32[]{:S(2)}) copy-start(f32[16,8,512]{2,1,0:T(8,128)} %param.9) | copy-start | bytes 786436
  0.7 20.3 %copy-start.1 = (f32[16,8,512]{2,1,0:T(8,128)S(1)}, f32[16,8,512]{2,1,0:T(8,128)}, u32[]{:S(2)}) copy-start(f32[16,8,512]{2,1,0:T(8,128)} %param.10) | copy-start | bytes 786436
  0.7 17.9 %copy-start = (f32[16,8,512]{2,1,0:T(8,128)S(1)}, f32[16,8,512]{2,1,0:T(8,128)}, u32[]{:S(2)}) copy-start(f32[16,8,512]{2,1,0:T(8,128)} %param.11) | copy-start | bytes 786436
  0.7 20.3 %copy-start.3 = (f32[16,8,512]{2,1,0:T(8,128)S(1)}, f32[16,8,512]{2,1,0:T(8,128)}, u32[]{:S(2)}) copy-start(f32[16,8,512]{2,1,0:T(8,128)} %param.8) | copy-start | bytes 786436
  0.7 20.3 %copy-start.5 = (f32[16,8,512]{2,1,0:T(8,128)S(1)}, f32[16,8,512]{2,1,0:T(8,128)}, u32[]{:S(2)}) copy-start(f32[16,8,512]{2,1,0:T(8,128)} %param.7) | copy-start | bytes 786436
  1.5 10.4 %collective-permute-start.2 = (f32[1,8,512]{2,1,0:T(8,128)S(1)}, f32[1,8,512]{2,1,0:T(8,128)S(1)}, u32[]{:S(2)}, u32[]{:S(2)}) collective-permute-start(f32[1,8,512]{2,1,0:T(8,128)S(1)} %get-tuple-element.35), channel_id=1, source_target_pairs={{0,8},{8,16},{16,24},{1,9},{9,17},{17,25},{2,10},{10,18},{18,26},{... | collective-permute-start | bytes 49160 | tf_op jit(solution)/shard_map/ppermute | solution.py:15
  7.1 11.6 %collective-permute-start = (f32[1,8,512]{2,1,0:T(8,128)S(1)}, f32[1,8,512]{2,1,0:T(8,128)S(1)}, u32[]{:S(2)}, u32[]{:S(2)}) collective-permute-start(f32[1,8,512]{2,1,0:T(8,128)S(1)} %slice.332), channel_id=1, source_target_pairs={{8,0},{16,8},{24,16},{9,1},{17,9},{25,17},{10,2},{18,10},{26,18},{... | collective-permute-start | bytes 49160 | tf_op jit(solution)/shard_map/ppermute | solution.py:26
  8.4 6.3 %collective-permute-start.3 = (f32[1,8,512]{2,1,0:T(8,128)S(1)}, f32[1,8,512]{2,1,0:T(8,128)S(1)}, u32[]{:S(2)}, u32[]{:S(2)}) collective-permute-start(f32[1,8,512]{2,1,0:T(8,128)S(1)} %get-tuple-element.34), channel_id=1, source_target_pairs={{8,0},{16,8},{24,16},{9,1},{17,9},{25,17},{10,2},{18,10},{26,18},{... | collective-permute-start | bytes 49160 | tf_op jit(solution)/shard_map/ppermute | solution.py:18
  10.7 8.0 %collective-permute-start.1 = (f32[16,1,512]{2,1,0:T(1,128)S(1)}, f32[16,1,512]{2,1,0:T(1,128)S(1)}, u32[]{:S(2)}, u32[]{:S(2)}) collective-permute-start(f32[16,1,512]{2,1,0:T(1,128)S(1)} %slice.334), channel_id=1, source_target_pairs={{1,0},{2,1},{3,2},{4,3},{5,4},{6,5},{7,6},{9,8},{10,9},{11,10},{12... | collective-permute-start | bytes 98312 | tf_op jit(solution)/shard_map/ppermute | solution.py:26
  14.7 4.0 %collective-permute-start.4 = (f32[18,1,512]{2,1,0:T(1,128)S(1)}, f32[18,1,512]{2,1,0:T(1,128)S(1)}, u32[]{:S(2)}, u32[]{:S(2)}) collective-permute-start(f32[18,1,512]{2,1,0:T(1,128)S(1)} %get-tuple-element.16), channel_id=1, source_target_pairs={{0,1},{1,2},{2,3},{3,4},{4,5},{5,6},{6,7},{8,9},{9,10},{10,11},{11... | collective-permute-start | bytes 110600 | tf_op jit(solution)/shard_map/ppermute | solution.py:15
  16.1 4.8 %collective-permute-start.5 = (f32[18,1,512]{2,1,0:T(1,128)S(1)}, f32[18,1,512]{2,1,0:T(1,128)S(1)}, u32[]{:S(2)}, u32[]{:S(2)}) collective-permute-start(f32[18,1,512]{2,1,0:T(1,128)S(1)} %get-tuple-element.17), channel_id=1, source_target_pairs={{1,0},{2,1},{3,2},{4,3},{5,4},{6,5},{7,6},{9,8},{10,9},{11,10},{12... | collective-permute-start | bytes 110600 | tf_op jit(solution)/shard_map/ppermute | solution.py:18
  66.7 5.6 %collective-permute-start.6 = (f32[1,8,512]{2,1,0:T(8,128)S(1)}, f32[1,8,512]{2,1,0:T(8,128)S(1)}, u32[]{:S(2)}, u32[]{:S(2)}) collective-permute-start(f32[1,8,512]{2,1,0:T(8,128)S(1)} %get-tuple-element.32), channel_id=1, source_target_pairs={{0,8},{8,16},{16,24},{1,9},{9,17},{17,25},{2,10},{10,18},{18,26},{... | collective-permute-start | bytes 49160 | tf_op jit(solution)/shard_map/ppermute | solution.py:15
  70.9 5.6 %collective-permute-start.7 = (f32[1,8,512]{2,1,0:T(8,128)S(1)}, f32[1,8,512]{2,1,0:T(8,128)S(1)}, u32[]{:S(2)}, u32[]{:S(2)}) collective-permute-start(f32[1,8,512]{2,1,0:T(8,128)S(1)} %get-tuple-element.33), channel_id=1, source_target_pairs={{8,0},{16,8},{24,16},{9,1},{17,9},{25,17},{10,2},{18,10},{26,18},{... | collective-permute-start | bytes 49160 | tf_op jit(solution)/shard_map/ppermute | solution.py:18
  76.6 2.7 %collective-permute-start.8 = (f32[18,1,512]{2,1,0:T(1,128)S(1)}, f32[18,1,512]{2,1,0:T(1,128)S(1)}, u32[]{:S(2)}, u32[]{:S(2)}) collective-permute-start(f32[18,1,512]{2,1,0:T(1,128)S(1)} %get-tuple-element.14), channel_id=1, source_target_pairs={{0,1},{1,2},{2,3},{3,4},{4,5},{5,6},{6,7},{8,9},{9,10},{10,11},{11... | collective-permute-start | bytes 110600 | tf_op jit(solution)/shard_map/ppermute | solution.py:15
  77.9 4.7 %collective-permute-start.9 = (f32[18,1,512]{2,1,0:T(1,128)S(1)}, f32[18,1,512]{2,1,0:T(1,128)S(1)}, u32[]{:S(2)}, u32[]{:S(2)}) collective-permute-start(f32[18,1,512]{2,1,0:T(1,128)S(1)} %get-tuple-element.15), channel_id=1, source_target_pairs={{1,0},{2,1},{3,2},{4,3},{5,4},{6,5},{7,6},{9,8},{10,9},{11,10},{12... | collective-permute-start | bytes 110600 | tf_op jit(solution)/shard_map/ppermute | solution.py:18
  82.9 5.9 %collective-permute-start.10 = (f32[1,8,512]{2,1,0:T(8,128)S(1)}, f32[1,8,512]{2,1,0:T(8,128)S(1)}, u32[]{:S(2)}, u32[]{:S(2)}) collective-permute-start(f32[1,8,512]{2,1,0:T(8,128)S(1)} %get-tuple-element.28), channel_id=1, source_target_pairs={{0,8},{8,16},{16,24},{1,9},{9,17},{17,25},{2,10},{10,18},{18,26},{... | collective-permute-start | bytes 49160 | tf_op jit(solution)/shard_map/ppermute | solution.py:15
  87.4 5.6 %collective-permute-start.11 = (f32[1,8,512]{2,1,0:T(8,128)S(1)}, f32[1,8,512]{2,1,0:T(8,128)S(1)}, u32[]{:S(2)}, u32[]{:S(2)}) collective-permute-start(f32[1,8,512]{2,1,0:T(8,128)S(1)} %get-tuple-element.29), channel_id=1, source_target_pairs={{8,0},{16,8},{24,16},{9,1},{17,9},{25,17},{10,2},{18,10},{26,18},{... | collective-permute-start | bytes 49160 | tf_op jit(solution)/shard_map/ppermute | solution.py:18
  93.1 4.6 %collective-permute-start.12 = (f32[18,1,512]{2,1,0:T(1,128)S(1)}, f32[18,1,512]{2,1,0:T(1,128)S(1)}, u32[]{:S(2)}, u32[]{:S(2)}) collective-permute-start(f32[18,1,512]{2,1,0:T(1,128)S(1)} %get-tuple-element.12), channel_id=1, source_target_pairs={{0,1},{1,2},{2,3},{3,4},{4,5},{5,6},{6,7},{8,9},{9,10},{10,11},{11... | collective-permute-start | bytes 110600 | tf_op jit(solution)/shard_map/ppermute | solution.py:15
  96.2 4.0 %collective-permute-start.13 = (f32[18,1,512]{2,1,0:T(1,128)S(1)}, f32[18,1,512]{2,1,0:T(1,128)S(1)}, u32[]{:S(2)}, u32[]{:S(2)}) collective-permute-start(f32[18,1,512]{2,1,0:T(1,128)S(1)} %get-tuple-element.13), channel_id=1, source_target_pairs={{1,0},{2,1},{3,2},{4,3},{5,4},{6,5},{7,6},{9,8},{10,9},{11,10},{12... | collective-permute-start | bytes 110600 | tf_op jit(solution)/shard_map/ppermute | solution.py:18
  100.6 4.3 %collective-permute-start.14 = (f32[1,8,512]{2,1,0:T(8,128)S(1)}, f32[1,8,512]{2,1,0:T(8,128)S(1)}, u32[]{:S(2)}, u32[]{:S(2)}) collective-permute-start(f32[1,8,512]{2,1,0:T(8,128)S(1)} %get-tuple-element.24), channel_id=1, source_target_pairs={{0,8},{8,16},{16,24},{1,9},{9,17},{17,25},{2,10},{10,18},{18,26},{... | collective-permute-start | bytes 49160 | tf_op jit(solution)/shard_map/ppermute | solution.py:15
  103.5 5.6 %collective-permute-start.15 = (f32[1,8,512]{2,1,0:T(8,128)S(1)}, f32[1,8,512]{2,1,0:T(8,128)S(1)}, u32[]{:S(2)}, u32[]{:S(2)}) collective-permute-start(f32[1,8,512]{2,1,0:T(8,128)S(1)} %get-tuple-element.25), channel_id=1, source_target_pairs={{8,0},{16,8},{24,16},{9,1},{17,9},{25,17},{10,2},{18,10},{26,18},{... | collective-permute-start | bytes 49160 | tf_op jit(solution)/shard_map/ppermute | solution.py:18
  109.1 4.6 %collective-permute-start.16 = (f32[18,1,512]{2,1,0:T(1,128)S(1)}, f32[18,1,512]{2,1,0:T(1,128)S(1)}, u32[]{:S(2)}, u32[]{:S(2)}) collective-permute-start(f32[18,1,512]{2,1,0:T(1,128)S(1)} %get-tuple-element.10), channel_id=1, source_target_pairs={{0,1},{1,2},{2,3},{3,4},{4,5},{5,6},{6,7},{8,9},{9,10},{10,11},{11... | collective-permute-start | bytes 110600 | tf_op jit(solution)/shard_map/ppermute | solution.py:15
  112.3 4.0 %collective-permute-start.17 = (f32[18,1,512]{2,1,0:T(1,128)S(1)}, f32[18,1,512]{2,1,0:T(1,128)S(1)}, u32[]{:S(2)}, u32[]{:S(2)}) collective-permute-start(f32[18,1,512]{2,1,0:T(1,128)S(1)} %get-tuple-element.11), channel_id=1, source_target_pairs={{1,0},{2,1},{3,2},{4,3},{5,4},{6,5},{7,6},{9,8},{10,9},{11,10},{12... | collective-permute-start | bytes 110600 | tf_op jit(solution)/shard_map/ppermute | solution.py:18
  116.7 5.0 %collective-permute-start.18 = (f32[1,8,512]{2,1,0:T(8,128)S(1)}, f32[1,8,512]{2,1,0:T(8,128)S(1)}, u32[]{:S(2)}, u32[]{:S(2)}) collective-permute-start(f32[1,8,512]{2,1,0:T(8,128)S(1)} %get-tuple-element.20), channel_id=1, source_target_pairs={{0,8},{8,16},{16,24},{1,9},{9,17},{17,25},{2,10},{10,18},{18,26},{... | collective-permute-start | bytes 49160 | tf_op jit(solution)/shard_map/ppermute | solution.py:15
  119.5 5.6 %collective-permute-start.19 = (f32[1,8,512]{2,1,0:T(8,128)S(1)}, f32[1,8,512]{2,1,0:T(8,128)S(1)}, u32[]{:S(2)}, u32[]{:S(2)}) collective-permute-start(f32[1,8,512]{2,1,0:T(8,128)S(1)} %get-tuple-element.21), channel_id=1, source_target_pairs={{8,0},{16,8},{24,16},{9,1},{17,9},{25,17},{10,2},{18,10},{26,18},{... | collective-permute-start | bytes 49160 | tf_op jit(solution)/shard_map/ppermute | solution.py:18
  125.2 4.9 %collective-permute-start.20 = (f32[18,1,512]{2,1,0:T(1,128)S(1)}, f32[18,1,512]{2,1,0:T(1,128)S(1)}, u32[]{:S(2)}, u32[]{:S(2)}) collective-permute-start(f32[18,1,512]{2,1,0:T(1,128)S(1)} %get-tuple-element.8), channel_id=1, source_target_pairs={{0,1},{1,2},{2,3},{3,4},{4,5},{5,6},{6,7},{8,9},{9,10},{10,11},{11... | collective-permute-start | bytes 110600 | tf_op jit(solution)/shard_map/ppermute | solution.py:15
  128.4 4.0 %collective-permute-start.21 = (f32[18,1,512]{2,1,0:T(1,128)S(1)}, f32[18,1,512]{2,1,0:T(1,128)S(1)}, u32[]{:S(2)}, u32[]{:S(2)}) collective-permute-start(f32[18,1,512]{2,1,0:T(1,128)S(1)} %get-tuple-element.9), channel_id=1, source_target_pairs={{1,0},{2,1},{3,2},{4,3},{5,4},{6,5},{7,6},{9,8},{10,9},{11,10},{12... | collective-permute-start | bytes 110600 | tf_op jit(solution)/shard_map/ppermute | solution.py:18
where the time goes:
time: 222 us; the launch traced here: 220 us
  blocking collectives  84.9 us (38%)
  starting transfers between devices  46.7 us (21%)
  between operations  34.1 us (15%)
  waiting for transfers between devices  31.1 us (14%)
  local copies, waits for them, and re-layouts  12.5 us (6%)
  matrix products  6.41 us (3%)
  other arithmetic  4.38 us (2%)
    psum x1, blocking collectives, local(): squares = lax.psum(jnp.sum(residual0 * residual0), ('gx', 'gy'))  44 us
    psum x1, blocking collectives, local(): gram = lax.psum(local_gram, ('gx', 'gy')) / cells  40.9 us
    ppermute x10, starting transfers between devices, padded(): lax.ppermute(lax.slice_in_dim(block, block.shape[dim] - width, None, axis...  31.2 us
    ppermute x10, waiting for transfers between devices, padded(): lax.ppermute(lax.slice_in_dim(block, 0, width, axis=dim), axis, backward)  30.7 us
    ppermute x10, starting transfers between devices, padded(): lax.ppermute(lax.slice_in_dim(block, 0, width, axis=dim), axis, backward)  12.9 us
    dot_general x1, matrix products, local(): jnp.einsum('axyz,bxyz->ab', block, block, precision=lax.Precision.HIGHEST)  4.56 us
  transfers between devices with their start and end apart: 22, of which 13 were waited for; matrix products, arithmetic and copies ran while one was open for 3% of the time, Pallas kernels for 0%

commit v1 on v0

--- a/solution.py
+++ b/solution.py
@@ -95,7 +95,7 @@
         basis.append(vector)
     block = jnp.stack(basis)
     local_gram = jnp.einsum("axyz,bxyz->ab", block, block, precision=lax.Precision.HIGHEST)
-    gram = lax.psum(local_gram, ("gx", "gy")) / cells
+    gram = lax.psum(lax.psum(local_gram, "gy"), "gx") / cells
     upper = jnp.linalg.cholesky(gram).T
     inverse = upper_inverse(upper)
     ortho = jnp.einsum("jk,jxyz->kxyz", inverse, block, precision=lax.Precision.HIGHEST)

time: 222 us -> 205 us (0.923)
  blocking collectives: 84.9 us -> 68.7 us
    psum x1 -> x2, blocking collectives: 40.9 us -> 24.6 us  [local(): gram = lax.psum(lax.psum(local_gram, 'gy'), 'gx') / cells]
where the time goes in v1:
time: 205 us; the launch traced here: 204 us
  blocking collectives  68.7 us (34%)
  starting transfers between devices  46.7 us (23%)
  between operations  34 us (17%)
  waiting for transfers between devices  31.1 us (15%)
  local copies, waits for them, and re-layouts  12.5 us (6%)
  matrix products  6.41 us (3%)
  other arithmetic  4.39 us (2%)
    psum x1, blocking collectives, local(): squares = lax.psum(jnp.sum(residual0 * residual0), ('gx', 'gy'))  44 us
    ppermute x10, starting transfers between devices, padded(): lax.ppermute(lax.slice_in_dim(block, block.shape[dim] - width, None, axis...  31.2 us
    ppermute x10, waiting for transfers between devices, padded(): lax.ppermute(lax.slice_in_dim(block, 0, width, axis=dim), axis, backward)  30.7 us
    psum x2, blocking collectives, local(): gram = lax.psum(lax.psum(local_gram, 'gy'), 'gx') / cells  24.6 us
    ppermute x10, starting transfers between devices, padded(): lax.ppermute(lax.slice_in_dim(block, 0, width, axis=dim), axis, backward)  12.9 us
    dot_general x1, matrix products, local(): jnp.einsum('axyz,bxyz->ab', block, block, precision=lax.Precision.HIGHEST)  4.56 us
  transfers between devices with their start and end apart: 22, of which 13 were waited for; matrix products, arithmetic and copies ran while one was open for 3% of the time, Pallas kernels for 0%

profile of v1, /device:TPU:0, one launch (start us, length us, event | category | flops | bytes accessed | tf_op | source)
XLA Modules:
  0.0 203.7 jit_solution(2842288891122812743)
XLA Ops:
  0.7 0.8 fusion.73
  1.5 4.8 %collective-permute-start.2 = (f32[1,8,512]{2,1,0:T(8,128)S(1)}, f32[1,8,512]{2,1,0:T(8,128)S(1)}, u32[]{:S(2)}, u32[]{:S(2)}) collective-permute-start(f32[1,8,512]{2,1,0:T(8,128)S(1)} %get-tuple-element.35), channel_id=1, source_target_pairs={{0,8},{8,16},{16,24},{1,9},{9,17},{17,25},{2,10},{10,18},{18,26},{... | collective-permute-start | bytes 49160 | tf_op jit(solution)/shard_map/ppermute | solution.py:15
  6.4 0.7 slice.332
  7.1 1.3 collective-permute-start
  8.4 1.3 collective-permute-start.3
  9.7 1.0 slice.334
  10.7 1.3 collective-permute-start.1
  12.0 1.0 constant_dynamic-update-slice_fusion.1
  13.0 1.7 collective-permute-done.3
  14.7 1.4 collective-permute-start.4
  16.1 1.3 collective-permute-start.5
  17.4 1.2 fusion.74
  18.7 2.2 %collective-permute-done.5 = f32[18,1,512]{2,1,0:T(1,128)S(1)} collective-permute-done((f32[18,1,512]{2,1,0:T(1,128)S(1)}, f32[18,1,512]{2,1,0:T(1,128)S(1)}, u32[]{:S(2)}, u32[]{:S(2)}) %collective-permute-start.5) | collective-permute-done | bytes 36896 | tf_op jit(solution)/shard_map/ppermute | solution.py:18
  21.0 1.0 multiply_reduce_fusion
  21.9 44.0 %psum.21 = f32[]{:T(128)} all-reduce(f32[]{:T(128)} %get-tuple-element.6), channel_id=1, replica_groups=mesh['gx'=4,'gy'=8] {'gx','gy'}, use_global_device_ids=true, to_apply=%region_1.2 | all-reduce | flops 1 | bytes 8 | tf_op jit(solution)/shard_map/psum | solution.py:88
  66.7 4.2 %collective-permute-start.6 = (f32[1,8,512]{2,1,0:T(8,128)S(1)}, f32[1,8,512]{2,1,0:T(8,128)S(1)}, u32[]{:S(2)}, u32[]{:S(2)}) collective-permute-start(f32[1,8,512]{2,1,0:T(8,128)S(1)} %get-tuple-element.32), channel_id=1, source_target_pairs={{0,8},{8,16},{16,24},{1,9},{9,17},{17,25},{2,10},{10,18},{18,26},{... | collective-permute-start | bytes 49160 | tf_op jit(solution)/shard_map/ppermute | solution.py:15
  70.9 1.3 collective-permute-start.7
  72.3 4.2 %collective-permute-done.7 = f32[1,8,512]{2,1,0:T(8,128)S(1)} collective-permute-done((f32[1,8,512]{2,1,0:T(8,128)S(1)}, f32[1,8,512]{2,1,0:T(8,128)S(1)}, u32[]{:S(2)}, u32[]{:S(2)}) %collective-permute-start.7) | collective-permute-done | bytes 16416 | tf_op jit(solution)/shard_map/ppermute | solution.py:18
  76.6 1.3 collective-permute-start.8
  77.9 1.3 collective-permute-start.9
  79.3 3.2 %collective-permute-done.9 = f32[18,1,512]{2,1,0:T(1,128)S(1)} collective-permute-done((f32[18,1,512]{2,1,0:T(1,128)S(1)}, f32[18,1,512]{2,1,0:T(1,128)S(1)}, u32[]{:S(2)}, u32[]{:S(2)}) %collective-permute-start.9) | collective-permute-done | bytes 36896 | tf_op jit(solution)/shard_map/ppermute | solution.py:18
  82.9 4.5 %collective-permute-start.10 = (f32[1,8,512]{2,1,0:T(8,128)S(1)}, f32[1,8,512]{2,1,0:T(8,128)S(1)}, u32[]{:S(2)}, u32[]{:S(2)}) collective-permute-start(f32[1,8,512]{2,1,0:T(8,128)S(1)} %get-tuple-element.28), channel_id=1, source_target_pairs={{0,8},{8,16},{16,24},{1,9},{9,17},{17,25},{2,10},{10,18},{18,26},{... | collective-permute-start | bytes 49160 | tf_op jit(solution)/shard_map/ppermute | solution.py:15
  87.4 1.3 collective-permute-start.11
  88.8 4.2 %collective-permute-done.11 = f32[1,8,512]{2,1,0:T(8,128)S(1)} collective-permute-done((f32[1,8,512]{2,1,0:T(8,128)S(1)}, f32[1,8,512]{2,1,0:T(8,128)S(1)}, u32[]{:S(2)}, u32[]{:S(2)}) %collective-permute-start.11) | collective-permute-done | bytes 16416 | tf_op jit(solution)/shard_map/ppermute | solution.py:18
  93.1 3.1 %collective-permute-start.12 = (f32[18,1,512]{2,1,0:T(1,128)S(1)}, f32[18,1,512]{2,1,0:T(1,128)S(1)}, u32[]{:S(2)}, u32[]{:S(2)}) collective-permute-start(f32[18,1,512]{2,1,0:T(1,128)S(1)} %get-tuple-element.12), channel_id=1, source_target_pairs={{0,1},{1,2},{2,3},{3,4},{4,5},{5,6},{6,7},{8,9},{9,10},{10,11},{11... | collective-permute-start | bytes 110600 | tf_op jit(solution)/shard_map/ppermute | solution.py:15
  96.2 1.3 collective-permute-start.13
  97.7 2.6 %collective-permute-done.13 = f32[18,1,512]{2,1,0:T(1,128)S(1)} collective-permute-done((f32[18,1,512]{2,1,0:T(1,128)S(1)}, f32[18,1,512]{2,1,0:T(1,128)S(1)}, u32[]{:S(2)}, u32[]{:S(2)}) %collective-permute-start.13) | collective-permute-done | bytes 36896 | tf_op jit(solution)/shard_map/ppermute | solution.py:18
  100.6 2.8 %collective-permute-start.14 = (f32[1,8,512]{2,1,0:T(8,128)S(1)}, f32[1,8,512]{2,1,0:T(8,128)S(1)}, u32[]{:S(2)}, u32[]{:S(2)}) collective-permute-start(f32[1,8,512]{2,1,0:T(8,128)S(1)} %get-tuple-element.24), channel_id=1, source_target_pairs={{0,8},{8,16},{16,24},{1,9},{9,17},{17,25},{2,10},{10,18},{18,26},{... | collective-permute-start | bytes 49160 | tf_op jit(solution)/shard_map/ppermute | solution.py:15
  103.5 1.3 collective-permute-start.15
  104.9 4.2 %collective-permute-done.15 = f32[1,8,512]{2,1,0:T(8,128)S(1)} collective-permute-done((f32[1,8,512]{2,1,0:T(8,128)S(1)}, f32[1,8,512]{2,1,0:T(8,128)S(1)}, u32[]{:S(2)}, u32[]{:S(2)}) %collective-permute-start.15) | collective-permute-done | bytes 16416 | tf_op jit(solution)/shard_map/ppermute | solution.py:18
  109.1 3.1 %collective-permute-start.16 = (f32[18,1,512]{2,1,0:T(1,128)S(1)}, f32[18,1,512]{2,1,0:T(1,128)S(1)}, u32[]{:S(2)}, u32[]{:S(2)}) collective-permute-start(f32[18,1,512]{2,1,0:T(1,128)S(1)} %get-tuple-element.10), channel_id=1, source_target_pairs={{0,1},{1,2},{2,3},{3,4},{4,5},{5,6},{6,7},{8,9},{9,10},{10,11},{11... | collective-permute-start | bytes 110600 | tf_op jit(solution)/shard_map/ppermute | solution.py:15
  112.3 1.3 collective-permute-start.17
  113.7 2.6 %collective-permute-done.17 = f32[18,1,512]{2,1,0:T(1,128)S(1)} collective-permute-done((f32[18,1,512]{2,1,0:T(1,128)S(1)}, f32[18,1,512]{2,1,0:T(1,128)S(1)}, u32[]{:S(2)}, u32[]{:S(2)}) %collective-permute-start.17) | collective-permute-done | bytes 36896 | tf_op jit(solution)/shard_map/ppermute | solution.py:18
  116.7 2.8 %collective-permute-start.18 = (f32[1,8,512]{2,1,0:T(8,128)S(1)}, f32[1,8,512]{2,1,0:T(8,128)S(1)}, u32[]{:S(2)}, u32[]{:S(2)}) collective-permute-start(f32[1,8,512]{2,1,0:T(8,128)S(1)} %get-tuple-element.20), channel_id=1, source_target_pairs={{0,8},{8,16},{16,24},{1,9},{9,17},{17,25},{2,10},{10,18},{18,26},{... | collective-permute-start | bytes 49160 | tf_op jit(solution)/shard_map/ppermute | solution.py:15
  119.5 1.3 collective-permute-start.19
  121.7 3.5 %collective-permute-done.19 = f32[1,8,512]{2,1,0:T(8,128)S(1)} collective-permute-done((f32[1,8,512]{2,1,0:T(8,128)S(1)}, f32[1,8,512]{2,1,0:T(8,128)S(1)}, u32[]{:S(2)}, u32[]{:S(2)}) %collective-permute-start.19) | collective-permute-done | bytes 16416 | tf_op jit(solution)/shard_map/ppermute | solution.py:18
  125.2 3.1 %collective-permute-start.20 = (f32[18,1,512]{2,1,0:T(1,128)S(1)}, f32[18,1,512]{2,1,0:T(1,128)S(1)}, u32[]{:S(2)}, u32[]{:S(2)}) collective-permute-start(f32[18,1,512]{2,1,0:T(1,128)S(1)} %get-tuple-element.8), channel_id=1, source_target_pairs={{0,1},{1,2},{2,3},{3,4},{4,5},{5,6},{6,7},{8,9},{9,10},{10,11},{11... | collective-permute-start | bytes 110600 | tf_op jit(solution)/shard_map/ppermute | solution.py:15
  128.4 1.3 collective-permute-start.21
  130.1 2.3 %collective-permute-done.21 = f32[18,1,512]{2,1,0:T(1,128)S(1)} collective-permute-done((f32[18,1,512]{2,1,0:T(1,128)S(1)}, f32[18,1,512]{2,1,0:T(1,128)S(1)}, u32[]{:S(2)}, u32[]{:S(2)}) %collective-permute-start.21) | collective-permute-done | bytes 36896 | tf_op jit(solution)/shard_map/ppermute | solution.py:18
  132.9 2.1 %stack.119 = f32[5,16,8,512]{3,0,2,1:T(8,128)S(1)} concatenate(f32[1,16,8,512]{3,0,2,1:T(1,128)S(1)} %copy.9, f32[1,16,8,512]{3,0,2,1:T(1,128)S(1)} %copy.10, f32[1,16,8,512]{3,0,2,1:T(1,128)S(1)} %copy.11, f32[1,16,8,512]{3,0,2,1:T(1,128)S(1)} %copy.12, f32[1,16,8,512]{3,0,2,1:T(1,128)S(1)} %stack.118), dimensions={0} | concatenate | bytes 2621440 | tf_op jit(solution)/shard_map/stack | solution.py:96
  135.0 4.6 %convolution_bitcast_fusion = f32[5,5]{0,1:T(8,128)S(1)} fusion(f32[5,16,8,512]{3,0,2,1:T(8,128)S(1)} %stack.119), kind=kOutput, calls=%fused_computation | convolution fusion | flops 19660800 | bytes 1310820 | tf_op jit(solution)/shard_map/axyz,bxyz->ab/dot_general | solution.py:97
  139.6 16.3 %psum.22 = f32[5,5]{0,1:T(8,128)S(1)} all-reduce(f32[5,5]{0,1:T(8,128)S(1)} %convolution_bitcast_fusion), channel_id=1, replica_groups=mesh['gx'=4,'gy'=8] {'gy'}, use_global_device_ids=true, to_apply=%region_2.3 | all-reduce | flops 25 | bytes 200 | tf_op jit(solution)/shard_map/psum | solution.py:98
  155.8 8.4 %psum.23 = f32[5,5]{0,1:T(8,128)S(1)} all-reduce(f32[5,5]{0,1:T(8,128)S(1)} %psum.22), channel_id=1, replica_groups=mesh['gx'=4,'gy'=8] {'gx'}, use_global_device_ids=true, to_apply=%region_3.4 | all-reduce | flops 25 | bytes 200 | tf_op jit(solution)/shard_map/psum | solution.py:98
  165.5 0.6 select_bitcast_fusion
  166.1 0.7 copy.16
  166.8 0.7 fusion.75
  198.9 1.8 fusion.60
  200.7 1.8 copy.15
  (63 shorter events, 5.7 us)
Async XLA Ops:
  0.6 20.3 %copy-start.4 = (f32[16,8,512]{2,1,0:T(8,128)S(1)}, f32[16,8,512]{2,1,0:T(8,128)}, u32[]{:S(2)}) copy-start(f32[16,8,512]{2,1,0:T(8,128)} %param.6) | copy-start | bytes 786436
  0.6 20.3 %copy-start.2 = (f32[16,8,512]{2,1,0:T(8,128)S(1)}, f32[16,8,512]{2,1,0:T(8,128)}, u32[]{:S(2)}) copy-start(f32[16,8,512]{2,1,0:T(8,128)} %param.9) | copy-start | bytes 786436
  0.7 20.3 %copy-start.1 = (f32[16,8,512]{2,1,0:T(8,128)S(1)}, f32[16,8,512]{2,1,0:T(8,128)}, u32[]{:S(2)}) copy-start(f32[16,8,512]{2,1,0:T(8,128)} %param.10) | copy-start | bytes 786436
  0.7 17.9 %copy-start = (f32[16,8,512]{2,1,0:T(8,128)S(1)}, f32[16,8,512]{2,1,0:T(8,128)}, u32[]{:S(2)}) copy-start(f32[16,8,512]{2,1,0:T(8,128)} %param.11) | copy-start | bytes 786436
  0.7 20.3 %copy-start.3 = (f32[16,8,512]{2,1,0:T(8,128)S(1)}, f32[16,8,512]{2,1,0:T(8,128)}, u32[]{:S(2)}) copy-start(f32[16,8,512]{2,1,0:T(8,128)} %param.8) | copy-start | bytes 786436
  0.7 20.3 %copy-start.5 = (f32[16,8,512]{2,1,0:T(8,128)S(1)}, f32[16,8,512]{2,1,0:T(8,128)}, u32[]{:S(2)}) copy-start(f32[16,8,512]{2,1,0:T(8,128)} %param.7) | copy-start | bytes 786436
  1.5 10.4 %collective-permute-start.2 = (f32[1,8,512]{2,1,0:T(8,128)S(1)}, f32[1,8,512]{2,1,0:T(8,128)S(1)}, u32[]{:S(2)}, u32[]{:S(2)}) collective-permute-start(f32[1,8,512]{2,1,0:T(8,128)S(1)} %get-tuple-element.35), channel_id=1, source_target_pairs={{0,8},{8,16},{16,24},{1,9},{9,17},{17,25},{2,10},{10,18},{18,26},{... | collective-permute-start | bytes 49160 | tf_op jit(solution)/shard_map/ppermute | solution.py:15
  7.1 11.6 %collective-permute-start = (f32[1,8,512]{2,1,0:T(8,128)S(1)}, f32[1,8,512]{2,1,0:T(8,128)S(1)}, u32[]{:S(2)}, u32[]{:S(2)}) collective-permute-start(f32[1,8,512]{2,1,0:T(8,128)S(1)} %slice.332), channel_id=1, source_target_pairs={{8,0},{16,8},{24,16},{9,1},{17,9},{25,17},{10,2},{18,10},{26,18},{... | collective-permute-start | bytes 49160 | tf_op jit(solution)/shard_map/ppermute | solution.py:26
  8.4 6.3 %collective-permute-start.3 = (f32[1,8,512]{2,1,0:T(8,128)S(1)}, f32[1,8,512]{2,1,0:T(8,128)S(1)}, u32[]{:S(2)}, u32[]{:S(2)}) collective-permute-start(f32[1,8,512]{2,1,0:T(8,128)S(1)} %get-tuple-element.34), channel_id=1, source_target_pairs={{8,0},{16,8},{24,16},{9,1},{17,9},{25,17},{10,2},{18,10},{26,18},{... | collective-permute-start | bytes 49160 | tf_op jit(solution)/shard_map/ppermute | solution.py:18
  10.7 8.0 %collective-permute-start.1 = (f32[16,1,512]{2,1,0:T(1,128)S(1)}, f32[16,1,512]{2,1,0:T(1,128)S(1)}, u32[]{:S(2)}, u32[]{:S(2)}) collective-permute-start(f32[16,1,512]{2,1,0:T(1,128)S(1)} %slice.334), channel_id=1, source_target_pairs={{1,0},{2,1},{3,2},{4,3},{5,4},{6,5},{7,6},{9,8},{10,9},{11,10},{12... | collective-permute-start | bytes 98312 | tf_op jit(solution)/shard_map/ppermute | solution.py:26
  14.7 4.0 %collective-permute-start.4 = (f32[18,1,512]{2,1,0:T(1,128)S(1)}, f32[18,1,512]{2,1,0:T(1,128)S(1)}, u32[]{:S(2)}, u32[]{:S(2)}) collective-permute-start(f32[18,1,512]{2,1,0:T(1,128)S(1)} %get-tuple-element.16), channel_id=1, source_target_pairs={{0,1},{1,2},{2,3},{3,4},{4,5},{5,6},{6,7},{8,9},{9,10},{10,11},{11... | collective-permute-start | bytes 110600 | tf_op jit(solution)/shard_map/ppermute | solution.py:15
  16.1 4.8 %collective-permute-start.5 = (f32[18,1,512]{2,1,0:T(1,128)S(1)}, f32[18,1,512]{2,1,0:T(1,128)S(1)}, u32[]{:S(2)}, u32[]{:S(2)}) collective-permute-start(f32[18,1,512]{2,1,0:T(1,128)S(1)} %get-tuple-element.17), channel_id=1, source_target_pairs={{1,0},{2,1},{3,2},{4,3},{5,4},{6,5},{7,6},{9,8},{10,9},{11,10},{12... | collective-permute-start | bytes 110600 | tf_op jit(solution)/shard_map/ppermute | solution.py:18
  66.7 5.6 %collective-permute-start.6 = (f32[1,8,512]{2,1,0:T(8,128)S(1)}, f32[1,8,512]{2,1,0:T(8,128)S(1)}, u32[]{:S(2)}, u32[]{:S(2)}) collective-permute-start(f32[1,8,512]{2,1,0:T(8,128)S(1)} %get-tuple-element.32), channel_id=1, source_target_pairs={{0,8},{8,16},{16,24},{1,9},{9,17},{17,25},{2,10},{10,18},{18,26},{... | collective-permute-start | bytes 49160 | tf_op jit(solution)/shard_map/ppermute | solution.py:15
  70.9 5.6 %collective-permute-start.7 = (f32[1,8,512]{2,1,0:T(8,128)S(1)}, f32[1,8,512]{2,1,0:T(8,128)S(1)}, u32[]{:S(2)}, u32[]{:S(2)}) collective-permute-start(f32[1,8,512]{2,1,0:T(8,128)S(1)} %get-tuple-element.33), channel_id=1, source_target_pairs={{8,0},{16,8},{24,16},{9,1},{17,9},{25,17},{10,2},{18,10},{26,18},{... | collective-permute-start | bytes 49160 | tf_op jit(solution)/shard_map/ppermute | solution.py:18
  76.6 2.7 %collective-permute-start.8 = (f32[18,1,512]{2,1,0:T(1,128)S(1)}, f32[18,1,512]{2,1,0:T(1,128)S(1)}, u32[]{:S(2)}, u32[]{:S(2)}) collective-permute-start(f32[18,1,512]{2,1,0:T(1,128)S(1)} %get-tuple-element.14), channel_id=1, source_target_pairs={{0,1},{1,2},{2,3},{3,4},{4,5},{5,6},{6,7},{8,9},{9,10},{10,11},{11... | collective-permute-start | bytes 110600 | tf_op jit(solution)/shard_map/ppermute | solution.py:15
  77.9 4.7 %collective-permute-start.9 = (f32[18,1,512]{2,1,0:T(1,128)S(1)}, f32[18,1,512]{2,1,0:T(1,128)S(1)}, u32[]{:S(2)}, u32[]{:S(2)}) collective-permute-start(f32[18,1,512]{2,1,0:T(1,128)S(1)} %get-tuple-element.15), channel_id=1, source_target_pairs={{1,0},{2,1},{3,2},{4,3},{5,4},{6,5},{7,6},{9,8},{10,9},{11,10},{12... | collective-permute-start | bytes 110600 | tf_op jit(solution)/shard_map/ppermute | solution.py:18
  82.9 5.9 %collective-permute-start.10 = (f32[1,8,512]{2,1,0:T(8,128)S(1)}, f32[1,8,512]{2,1,0:T(8,128)S(1)}, u32[]{:S(2)}, u32[]{:S(2)}) collective-permute-start(f32[1,8,512]{2,1,0:T(8,128)S(1)} %get-tuple-element.28), channel_id=1, source_target_pairs={{0,8},{8,16},{16,24},{1,9},{9,17},{17,25},{2,10},{10,18},{18,26},{... | collective-permute-start | bytes 49160 | tf_op jit(solution)/shard_map/ppermute | solution.py:15
  87.4 5.6 %collective-permute-start.11 = (f32[1,8,512]{2,1,0:T(8,128)S(1)}, f32[1,8,512]{2,1,0:T(8,128)S(1)}, u32[]{:S(2)}, u32[]{:S(2)}) collective-permute-start(f32[1,8,512]{2,1,0:T(8,128)S(1)} %get-tuple-element.29), channel_id=1, source_target_pairs={{8,0},{16,8},{24,16},{9,1},{17,9},{25,17},{10,2},{18,10},{26,18},{... | collective-permute-start | bytes 49160 | tf_op jit(solution)/shard_map/ppermute | solution.py:18
  93.1 4.6 %collective-permute-start.12 = (f32[18,1,512]{2,1,0:T(1,128)S(1)}, f32[18,1,512]{2,1,0:T(1,128)S(1)}, u32[]{:S(2)}, u32[]{:S(2)}) collective-permute-start(f32[18,1,512]{2,1,0:T(1,128)S(1)} %get-tuple-element.12), channel_id=1, source_target_pairs={{0,1},{1,2},{2,3},{3,4},{4,5},{5,6},{6,7},{8,9},{9,10},{10,11},{11... | collective-permute-start | bytes 110600 | tf_op jit(solution)/shard_map/ppermute | solution.py:15
  96.2 4.0 %collective-permute-start.13 = (f32[18,1,512]{2,1,0:T(1,128)S(1)}, f32[18,1,512]{2,1,0:T(1,128)S(1)}, u32[]{:S(2)}, u32[]{:S(2)}) collective-permute-start(f32[18,1,512]{2,1,0:T(1,128)S(1)} %get-tuple-element.13), channel_id=1, source_target_pairs={{1,0},{2,1},{3,2},{4,3},{5,4},{6,5},{7,6},{9,8},{10,9},{11,10},{12... | collective-permute-start | bytes 110600 | tf_op jit(solution)/shard_map/ppermute | solution.py:18
  100.6 4.3 %collective-permute-start.14 = (f32[1,8,512]{2,1,0:T(8,128)S(1)}, f32[1,8,512]{2,1,0:T(8,128)S(1)}, u32[]{:S(2)}, u32[]{:S(2)}) collective-permute-start(f32[1,8,512]{2,1,0:T(8,128)S(1)} %get-tuple-element.24), channel_id=1, source_target_pairs={{0,8},{8,16},{16,24},{1,9},{9,17},{17,25},{2,10},{10,18},{18,26},{... | collective-permute-start | bytes 49160 | tf_op jit(solution)/shard_map/ppermute | solution.py:15
  103.5 5.6 %collective-permute-start.15 = (f32[1,8,512]{2,1,0:T(8,128)S(1)}, f32[1,8,512]{2,1,0:T(8,128)S(1)}, u32[]{:S(2)}, u32[]{:S(2)}) collective-permute-start(f32[1,8,512]{2,1,0:T(8,128)S(1)} %get-tuple-element.25), channel_id=1, source_target_pairs={{8,0},{16,8},{24,16},{9,1},{17,9},{25,17},{10,2},{18,10},{26,18},{... | collective-permute-start | bytes 49160 | tf_op jit(solution)/shard_map/ppermute | solution.py:18
  109.1 4.6 %collective-permute-start.16 = (f32[18,1,512]{2,1,0:T(1,128)S(1)}, f32[18,1,512]{2,1,0:T(1,128)S(1)}, u32[]{:S(2)}, u32[]{:S(2)}) collective-permute-start(f32[18,1,512]{2,1,0:T(1,128)S(1)} %get-tuple-element.10), channel_id=1, source_target_pairs={{0,1},{1,2},{2,3},{3,4},{4,5},{5,6},{6,7},{8,9},{9,10},{10,11},{11... | collective-permute-start | bytes 110600 | tf_op jit(solution)/shard_map/ppermute | solution.py:15
  112.3 4.0 %collective-permute-start.17 = (f32[18,1,512]{2,1,0:T(1,128)S(1)}, f32[18,1,512]{2,1,0:T(1,128)S(1)}, u32[]{:S(2)}, u32[]{:S(2)}) collective-permute-start(f32[18,1,512]{2,1,0:T(1,128)S(1)} %get-tuple-element.11), channel_id=1, source_target_pairs={{1,0},{2,1},{3,2},{4,3},{5,4},{6,5},{7,6},{9,8},{10,9},{11,10},{12... | collective-permute-start | bytes 110600 | tf_op jit(solution)/shard_map/ppermute | solution.py:18
  116.7 5.0 %collective-permute-start.18 = (f32[1,8,512]{2,1,0:T(8,128)S(1)}, f32[1,8,512]{2,1,0:T(8,128)S(1)}, u32[]{:S(2)}, u32[]{:S(2)}) collective-permute-start(f32[1,8,512]{2,1,0:T(8,128)S(1)} %get-tuple-element.20), channel_id=1, source_target_pairs={{0,8},{8,16},{16,24},{1,9},{9,17},{17,25},{2,10},{10,18},{18,26},{... | collective-permute-start | bytes 49160 | tf_op jit(solution)/shard_map/ppermute | solution.py:15
  119.5 5.6 %collective-permute-start.19 = (f32[1,8,512]{2,1,0:T(8,128)S(1)}, f32[1,8,512]{2,1,0:T(8,128)S(1)}, u32[]{:S(2)}, u32[]{:S(2)}) collective-permute-start(f32[1,8,512]{2,1,0:T(8,128)S(1)} %get-tuple-element.21), channel_id=1, source_target_pairs={{8,0},{16,8},{24,16},{9,1},{17,9},{25,17},{10,2},{18,10},{26,18},{... | collective-permute-start | bytes 49160 | tf_op jit(solution)/shard_map/ppermute | solution.py:18
  125.2 4.9 %collective-permute-start.20 = (f32[18,1,512]{2,1,0:T(1,128)S(1)}, f32[18,1,512]{2,1,0:T(1,128)S(1)}, u32[]{:S(2)}, u32[]{:S(2)}) collective-permute-start(f32[18,1,512]{2,1,0:T(1,128)S(1)} %get-tuple-element.8), channel_id=1, source_target_pairs={{0,1},{1,2},{2,3},{3,4},{4,5},{5,6},{6,7},{8,9},{9,10},{10,11},{11... | collective-permute-start | bytes 110600 | tf_op jit(solution)/shard_map/ppermute | solution.py:15
  128.4 4.0 %collective-permute-start.21 = (f32[18,1,512]{2,1,0:T(1,128)S(1)}, f32[18,1,512]{2,1,0:T(1,128)S(1)}, u32[]{:S(2)}, u32[]{:S(2)}) collective-permute-start(f32[18,1,512]{2,1,0:T(1,128)S(1)} %get-tuple-element.9), channel_id=1, source_target_pairs={{1,0},{2,1},{3,2},{4,3},{5,4},{6,5},{7,6},{9,8},{10,9},{11,10},{12... | collective-permute-start | bytes 110600 | tf_op jit(solution)/shard_map/ppermute | solution.py:18
